TPU v7x, 512 devices: a whole 4x8x8 slice. The times are simulated.
512 devices in a mesh: row: 32 (over x, z), col: 16 (over y, core).
Axes of the slice: x: 4, y: 8, z: 8, core: 2. Of those that a mesh axis runs over, the one named last changes fastest.
Arguments:
- matrix: float32 [14336, 14336], P('row', 'col'), may hold values from -3 to 3
- reflectors: float32 [1, 64, 14336], P(None, None, 'row'), may hold values from -0.09375 to 0.09375
- factors: float32 [1, 64, 64], replicated, may hold values from -0.1 to 2, as said below
Outputs:
- updated: float32 [14336, 14336], P('row', 'col')
- companions: float32 [1, 64, 14336], P(None, None, 'row')
Inputs may be any that keep to these rules, and one draw needn't show every extreme that they name: `factors`: each factor is upper triangular (zero below the diagonal) with diagonal entries between 1 and 2.
All inputs are finite; a program needn't handle non-finite values.
Results may differ from a plain program's by a relative error of at most 0.0001.
Values sent between devices are 32-bit elements; how exact they have to be, the bound alone decides.
No kernel may reach another device: no remote copies, remote signals or barrier semaphores. Data moves between devices by JAX's collectives and lax.ppermute only.
A program may use at most 64 MiB of HBM per device.

v0:
```python
import jax
import jax.numpy as jnp
from jax import lax
from jax.sharding import PartitionSpec as P


def spread(block, axis, owner):
    block = jnp.where(lax.axis_index(axis) == owner, block, jnp.zeros_like(block))
    return lax.psum(block, axis)


def contract(left_side, right_side, left_dim, right_dim):
    return lax.dot_general(
        left_side,
        right_side,
        (((left_dim,), (right_dim,)), ((), ())),
        precision=lax.Precision.HIGHEST,
        preferred_element_type=jnp.float32,
    )


def reflector_blocks(values):
    group_ratio = lax.axis_size("row") // lax.axis_size("col")
    column = lax.axis_index("col")
    pieces = []
    for offset in range(group_ratio):
        root_index = column * group_ratio + offset
        pieces.append(spread(values, "row", root_index))
    return jnp.concatenate(pieces, axis=values.ndim - 1)


def shards(matrix, reflectors, factors):
    current = matrix
    reflector_cols = reflector_blocks(reflectors)
    v_rows = reflectors[0]
    v_cols = reflector_cols[0]
    factor = factors[0]
    partial_value = contract(v_cols, current, 1, 1)
    column_partial = contract(v_rows, current, 1, 0)
    row_sums = lax.psum(partial_value, "col")
    x_rows = contract(factor, row_sums, 0, 0)
    projected = lax.psum(contract(v_rows, x_rows, 1, 1), "row")
    mixing = contract(projected, factor, 0, 0)
    w_rows = x_rows - 0.5 * contract(mixing, v_rows, 1, 0)
    col_sums = lax.psum(column_partial, "row")
    x_cols = contract(factor, col_sums, 0, 0)
    w_cols = x_cols - 0.5 * contract(mixing, v_cols, 1, 0)
    current = current - contract(v_rows, w_cols, 0, 0) - contract(w_rows, v_cols, 0, 0)
    results = [w_rows]
    return (current, jnp.stack(results))


def solution(mesh):
    return jax.shard_map(
        shards,
        mesh=mesh,
        in_specs=(P("row", "col"), P(None, None, "row"), P()),
        out_specs=(P("row", "col"), P(None, None, "row")),
        check_vma=False,
    )
```

profile of v0, /device:TPU:24, one launch (start us, length us, event | category | flops | bytes accessed | tf_op | source)
XLA Modules:
  0.0 447.1 jit_solution(9648008019465141000)
XLA Ops:
  7.2 0.0 copy-start
  7.2 0.0 copy-start.2
  7.2 0.0 copy-start.1
  7.2 0.0 all-reduce.6.cloned.1.call-start
  7.3 3.3 fusion.7
  10.6 0.0 copy-done.2
  10.6 0.7 broadcast_select_fusion.1
  11.3 0.0 all-reduce.6.cloned.1.call-update
  11.3 0.0 all-reduce.4.cloned.1.call-start
  11.4 164.7 %all-reduce.6.cloned.1.call-done = (f32[1,64,448]{2,1,0:T(8,128)}, f32[1,64,448]{2,1,0:T(8,128)}, f32[64,896]{1,0:T(8,128)}) async-done(((f32[1,64,448]{2,1,0:T(8,128)}, f32[1,64,448]{2,1,0:T(8,128)}, f32[64,896]{1,0:T(8,128)}), (f32[1,64,448]{2,1,0:T(8,128)}, f32[1,64,448]{2,1,0:T(8,128)}, f32[64,896]{1,0:T(8,128)})) %all-reduce.6.cloned.1.call-update) | async-done | bytes 458768 | tf_op jit(solution)/shard_map/psum | solution.py:9
  176.0 0.0 copy-done.1
  176.0 0.0 copy-start.3
  176.0 0.0 copy-start.4
  176.0 0.0 copy-start.6
  176.1 3.3 fusion.9
  179.4 0.0 all-reduce.4.cloned.1.call-update
  179.4 109.2 %all-reduce.4.cloned.1.call-done = f32[64,448]{1,0:T(8,128)} async-done(((f32[64,448]{1,0:T(8,128)}), f32[64,448]{1,0:T(8,128)}) %all-reduce.4.cloned.1.call-update) | async-done | bytes 114704 | tf_op jit(solution)/shard_map/psum | solution.py:40
  288.6 0.0 copy-done
  288.6 1.2 fusion.12
  289.8 0.3 convolution_bitcast_fusion.1
  290.1 143.7 %psum.39 = f32[64,64]{0,1:T(8,128)S(1)} all-reduce(f32[64,64]{0,1:T(8,128)S(1)} %convolution_bitcast_fusion.1), channel_id=1, replica_groups=mesh['row'=32,'col'=16] {'row'}, use_global_device_ids=true, to_apply=%region_4.5 | all-reduce | flops 4096 | bytes 32768 | tf_op jit(solution)/shard_map/psum | solution.py:42
  433.8 0.2 fusion.10
  434.0 0.3 fusion.2
  434.2 0.0 copy-done.3
  434.2 0.0 copy-done.4
  434.2 0.0 copy-start.5
  434.3 1.0 convolution_multiply_fusion
  435.2 0.0 copy-done.6
  435.2 0.9 fusion.1
  436.2 1.5 fusion.4
  437.6 0.0 copy-done.5
  437.6 2.6 fusion
Async XLA Ops:
  7.2 281.4 %copy-start = (f32[1,64,64]{2,1,0:T(8,128)S(1)}, f32[1,64,64]{2,1,0:T(8,128)}, u32[]{:S(2)}) copy-start(f32[1,64,64]{2,1,0:T(8,128)} %param.5) | copy-start | bytes 49156
  7.2 3.4 copy-start.2
  7.2 168.9 %copy-start.1 = (f32[448,896]{1,0:T(8,128)S(1)}, f32[448,896]{1,0:T(8,128)}, u32[]{:S(2)}) copy-start(f32[448,896]{1,0:T(8,128)} %param.3) | copy-start | bytes 4816900
  7.2 168.8 %all-reduce.6.cloned.1.call-start = ((), (), s32[]{:S(2)}) async-start(), calls=%async_computation.1 | async-start | bytes 983040 | tf_op jit(solution)/shard_map/psum | solution.py:9
  11.3 277.2 %all-reduce.4.cloned.1.call-start = ((), (), s32[]{:S(2)}) async-start(), calls=%async_computation | async-start | bytes 262144 | tf_op jit(solution)/shard_map/psum | solution.py:40
  176.0 258.2 %copy-start.3 = (f32[1,64,448]{2,1,0:T(8,128)S(1)}, f32[1,64,448]{2,1,0:T(8,128)}, u32[]{:S(2)}) copy-start(f32[1,64,448]{2,1,0:T(8,128)} %get-tuple-element.2) | copy-start | bytes 344068
  176.0 258.2 %copy-start.4 = (f32[1,64,448]{2,1,0:T(8,128)S(1)}, f32[1,64,448]{2,1,0:T(8,128)}, u32[]{:S(2)}) copy-start(f32[1,64,448]{2,1,0:T(8,128)} %get-tuple-element.3) | copy-start | bytes 344068
  176.0 259.2 %copy-start.6 = (f32[64,896]{1,0:T(8,128)S(1)}, f32[64,896]{1,0:T(8,128)}, u32[]{:S(2)}) copy-start(f32[64,896]{1,0:T(8,128)} %get-tuple-element.4) | copy-start | bytes 688132
  434.2 3.4 copy-start.5
Sparse Core Ops, SparseCore 0:
  12.3 163.7 all-reduce.5
  179.5 108.9 all-reduce.3
where the time goes:
time: 447 us
  waiting for transfers between devices  274 us (61%)
  blocking collectives  144 us (32%)
  matrix products  14.5 us (3%)
  between operations  14.2 us (3%)
    psum x1, waiting for transfers between devices, spread(): return lax.psum(block, axis)  165 us
    psum x1, blocking collectives, shards(): projected = lax.psum(contract(v_rows, x_rows, 1, 1), 'row')  144 us
    psum x1, waiting for transfers between devices, shards(): row_sums = lax.psum(partial_value, 'col')  109 us
    dot_general x10, matrix products, contract(): lax.dot_general(left_side, right_side, (((left_dim,), (right_dim,)), ((),...  14.5 us
  transfers between devices with their start and end apart: 2, of which 2 were waited for; matrix products, arithmetic and copies ran while one was open for 0% of the time, Pallas kernels for 0%

commit v1 on v0

--- a/solution.py
+++ b/solution.py
@@ -6,7 +6,11 @@
 
 def spread(block, axis, owner):
     block = jnp.where(lax.axis_index(axis) == owner, block, jnp.zeros_like(block))
-    return lax.psum(block, axis)
+
+    def attach_slices(local_block):
+        return jnp.sum(jax.lax.all_gather(local_block, axis_name=axis), 0)
+
+    return attach_slices(block)
 
 
 def contract(left_side, right_side, left_dim, right_dim):

time: 447 us -> 480 us (1.074)
  the two profiles are of different devices: /device:TPU:24 before, /device:TPU:8 now
where the time goes in v1:
time: 480 us
  waiting for transfers between devices  303 us (63%)
  blocking collectives  143 us (30%)
  between operations  13.9 us (3%)
  matrix products  12.9 us (3%)
  other arithmetic  6.77 us (1%)
    all_gather x2, waiting for transfers between devices, attach_slices(): return jnp.sum(jax.lax.all_gather(local_block, axis_name=axis), 0)  181 us
    psum x1, blocking collectives, shards(): projected = lax.psum(contract(v_rows, x_rows, 1, 1), 'row')  143 us
    psum x1, waiting for transfers between devices, shards(): row_sums = lax.psum(partial_value, 'col')  106 us
    psum x1, waiting for transfers between devices, shards(): col_sums = lax.psum(column_partial, 'row')  15.7 us
    dot_general x10, matrix products, contract(): lax.dot_general(left_side, right_side, (((left_dim,), (right_dim,)), ((),...  12.9 us
  transfers between devices with their start and end apart: 4, of which 4 were waited for; matrix products, arithmetic and copies ran while one was open for 1% of the time, Pallas kernels for 0%

profile of v1, /device:TPU:8, one launch (start us, length us, event | category | flops | bytes accessed | tf_op | source)
XLA Modules:
  0.0 479.7 jit_solution(8924333056804101091)
XLA Ops:
  7.2 0.0 copy-start
  7.2 0.0 all-gather.5.cloned.1.call-start
  7.2 1.6 broadcast_select_fusion.1
  8.9 0.0 all-gather.5.cloned.1.call-update
  8.9 0.0 all-gather.7.cloned.1.call-start
  8.9 0.7 all-gather.7.cloned.1.call-update
  9.6 0.0 all-reduce.5.cloned.1.call-start
  9.7 95.1 %all-gather.5.cloned.1.call-done = f32[32,64,448]{2,1,0:T(8,128)} async-done(((f32[1,64,448]{2,1,0:T(8,128)}), f32[32,64,448]{2,1,0:T(8,128)}) %all-gather.5.cloned.1.call-update) | async-done | bytes 3670032 | tf_op jit(solution)/shard_map/all_gather | solution.py:11
  104.8 2.6 reduce.2
  107.4 0.0 copy-start.1
  107.4 85.9 %all-gather.7.cloned.1.call-done = f32[32,64,448]{2,1,0:T(8,128)} async-done(((f32[1,64,448]{2,1,0:T(8,128)}), f32[32,64,448]{2,1,0:T(8,128)}) %all-gather.7.cloned.1.call-update) | async-done | bytes 3670032 | tf_op jit(solution)/shard_map/all_gather | solution.py:11
  193.3 2.6 reduce.3
  195.9 0.0 copy-start.2
  195.9 0.0 copy-done.1
  195.9 2.3 fusion.9
  198.2 0.0 all-reduce.5.cloned.1.call-update
  198.2 0.0 all-reduce.3.cloned.1.call-start
  198.3 0.0 copy-done.2
  198.3 1.7 fusion.7
  200.0 0.0 all-reduce.3.cloned.1.call-update
  200.0 105.7 %all-reduce.5.cloned.1.call-done = f32[64,448]{1,0:T(8,128)} async-done(((f32[64,448]{1,0:T(8,128)}), f32[64,448]{1,0:T(8,128)}) %all-reduce.5.cloned.1.call-update) | async-done | bytes 114704 | tf_op jit(solution)/shard_map/psum | solution.py:44
  305.7 0.0 copy-done
  305.7 1.2 fusion.12
  306.9 0.3 convolution_bitcast_fusion.1
  307.2 142.9 %psum.23 = f32[64,64]{0,1:T(8,128)S(1)} all-reduce(f32[64,64]{0,1:T(8,128)S(1)} %convolution_bitcast_fusion.1), channel_id=1, replica_groups=mesh['row'=32,'col'=16] {'row'}, use_global_device_ids=true, to_apply=%region_4.5 | all-reduce | flops 4096 | bytes 32768 | tf_op jit(solution)/shard_map/psum | solution.py:46
  450.1 0.2 fusion.10
  450.3 1.0 convolution_multiply_fusion
  451.3 0.3 fusion.2
  451.6 0.0 copy-start.3
  451.6 15.7 %all-reduce.3.cloned.1.call-done = f32[64,896]{1,0:T(8,128)} async-done(((f32[64,896]{1,0:T(8,128)}), f32[64,896]{1,0:T(8,128)}) %all-reduce.3.cloned.1.call-update) | async-done | bytes 229392 | tf_op jit(solution)/shard_map/psum | solution.py:49
  467.2 1.8 fusion.1
  469.1 1.5 fusion.4
  470.5 0.0 copy-done.3
  470.5 2.7 fusion
Async XLA Ops:
  7.2 298.5 %copy-start = (f32[1,64,64]{2,1,0:T(8,128)S(1)}, f32[1,64,64]{2,1,0:T(8,128)}, u32[]{:S(2)}) copy-start(f32[1,64,64]{2,1,0:T(8,128)} %param.5) | copy-start | bytes 49156
  7.2 97.6 %all-gather.5.cloned.1.call-start = ((), (), s32[]{:S(2)}) async-start(), calls=%async_computation.2 | async-start | bytes 4325376 | tf_op jit(solution)/shard_map/all_gather | solution.py:11
  8.9 184.4 %all-gather.7.cloned.1.call-start = ((), (), s32[]{:S(2)}) async-start(), calls=%async_computation.3 | async-start | bytes 4325376 | tf_op jit(solution)/shard_map/all_gather | solution.py:11
  9.6 296.1 %all-reduce.5.cloned.1.call-start = ((), (), s32[]{:S(2)}) async-start(), calls=%async_computation.1 | async-start | bytes 262144 | tf_op jit(solution)/shard_map/psum | solution.py:44
  107.4 88.5 %copy-start.1 = (f32[448,896]{1,0:T(8,128)S(1)}, f32[448,896]{1,0:T(8,128)}, u32[]{:S(2)}) copy-start(f32[448,896]{1,0:T(8,128)} %param.3) | copy-start | bytes 4816900
  195.9 2.4 copy-start.2
  198.2 269.0 %all-reduce.3.cloned.1.call-start = ((), (), s32[]{:S(2)}) async-start(), calls=%async_computation | async-start | bytes 458752 | tf_op jit(solution)/shard_map/psum | solution.py:49
  451.6 19.0 %copy-start.3 = (f32[64,448]{1,0:T(8,128)}, f32[64,448]{1,0:T(8,128)S(1)}, u32[]{:S(2)}) copy-start(f32[64,448]{1,0:T(8,128)S(1)} %fusion.2) | copy-start | bytes 344068
Sparse Core Ops, SparseCore 0:
  11.8 93.0 all-gather.4
  108.6 84.6 all-gather.6
  198.4 107.2 all-reduce.4
  310.0 157.2 all-reduce.2
